TPU v7x, 32 devices: a whole 2x2x4 slice. The times are simulated.
32 devices in a mesh: section: 2 (over x), mp: 4 (over z), dp: 4 (over y, core).
Axes of the slice: x: 2, y: 2, z: 4, core: 2. Of those that a mesh axis runs over, the one named last changes fastest.
Arguments:
- text_in: bfloat16 [4, 2, 512, 8192], P('dp', 'section', None, 'mp'), may hold values from -6 to 6
- vision: bfloat16 [4, 2, 256, 8192], P('dp', 'section', None, 'mp'), may hold values from -6 to 6
- tile_counts: int32 [4, 2], P('dp'), may hold values from 1 to 4, as said below
- lengths: int32 [4, 2], P('dp', 'section'), may hold values from 128 to 512, as said below
- image_of: int32 [4, 2], P('dp'), may hold values from 0 to 1, each once within a row
- norm_gain: float32 [2, 8192], P('section'), may hold values from 0.5 to 1.5
- query_weight: bfloat16 [2, 8192, 4096], P('section', 'dp', 'mp'), may hold values from -0.0625 to 0.0625
- key_weight: bfloat16 [2, 8192, 1024], P('section', 'dp', 'mp'), may hold values from -0.0625 to 0.0625
- value_weight: bfloat16 [2, 8192, 1024], P('section', 'dp', 'mp'), may hold values from -0.0625 to 0.0625
- query_gain: float32 [2, 128], P('section')
- key_gain: float32 [2, 128], P('section')
- cross_gate: float32 [2], P('section'), may hold values from 0.4 to 1.5
- context_grad: bfloat16 [4, 2, 512, 4096], P('dp', 'section', None, 'mp'), may hold values from -6 to 6
Outputs:
- gated_context: bfloat16 [4, 2, 512, 4096], P('dp', 'section', None, 'mp')
- vision_grad: bfloat16 [4, 2, 256, 8192], P('dp', 'section', None, 'mp')
- key_weight_grad: bfloat16 [2, 8192, 1024], P('section', 'dp', 'mp')
- value_weight_grad: bfloat16 [2, 8192, 1024], P('section', 'dp', 'mp')
Inputs may be any that keep to these rules, and one draw needn't show every extreme that they name: `tile_counts`: some image has 4 tiles and some has one. `lengths`: some sample has the full 512 tokens. `image_of`: each row is a permutation of the sections.
All inputs are finite; a program needn't handle non-finite values.
Results may differ from a plain program's by a relative error of at most 0.018.
Values may be sent and summed in bfloat16 or wider, within the bound.
No kernel may reach another device: no remote copies, remote signals or barrier semaphores. Data moves between devices by JAX's collectives and lax.ppermute only.
A program may use at most 192 MiB of HBM per device.

v0:
```python
import jax
import jax.numpy as jnp
from jax import lax
from jax.sharding import PartitionSpec as P

HD = 128
TILE_ROWS = 64


def shifted(value, axis, steps):
    count = lax.axis_size(axis)
    pairs = [(source, (source + steps) % count) for source in range(count)]
    return lax.ppermute(value, axis, pairs)


def norm_rows(values, gain):
    values = values.astype(jnp.float32)
    scaled = values * lax.rsqrt(jnp.mean(values * values, axis=-1, keepdims=True) + 1e-05)
    return scaled * gain


def rounded(values):
    return lax.optimization_barrier(values.astype(jnp.bfloat16)).astype(jnp.float32)


def attend(queries, keys_raw, values_raw, key_norm, usable, present, gate_value):
    keys = rounded(norm_rows(keys_raw, key_norm))
    values = rounded(values_raw)
    text_rows, heads, depth = queries.shape
    groups = keys.shape[1]
    grouped = queries.astype(jnp.float32).reshape(text_rows, groups, heads // groups, depth)
    scores = jnp.einsum("tgjd,vgd->gjtv", grouped, keys) * depth ** (-0.5)
    scores = jnp.where(usable[None, None, None, :], scores, -1e30)
    highest = lax.stop_gradient(jnp.max(scores, axis=-1, keepdims=True))
    weights = jnp.exp(scores - highest)
    probs = rounded(weights / jnp.sum(weights, axis=-1, keepdims=True))
    context = jnp.einsum("gjtv,vgd->tgjd", probs, values).reshape(text_rows, heads * depth)
    return jnp.where(present[:, None], jnp.tanh(gate_value) * context, 0.0)


def per_device(
    text_in,
    vision,
    tile_counts,
    lengths,
    image_of,
    norm_gain,
    query_weight,
    key_weight,
    value_weight,
    query_gain,
    key_gain,
    cross_gate,
    context_grad,
):
    arrived = shifted(text_in, "section", 1)
    full_text = lax.all_gather(arrived, "mp", axis=3, tiled=True)[0, 0]
    text_rows = full_text.shape[0]
    normed = norm_rows(full_text, norm_gain[0]).astype(jnp.bfloat16)
    width_q = query_weight.shape[2]
    columns = normed
    query_raw = jnp.dot(
        columns,
        lax.all_gather(query_weight, "dp", axis=1, tiled=True)[0],
        preferred_element_type=jnp.float32,
    )
    queries = norm_rows(query_raw.reshape(text_rows, width_q // HD, HD), query_gain[0]).astype(
        jnp.bfloat16
    )
    key_full, value_full = (
        lax.all_gather(key_weight, "dp", axis=1, tiled=True),
        lax.all_gather(value_weight, "dp", axis=1, tiled=True),
    )
    key_full = key_full[0]
    value_full = value_full[0]
    slot_rows = vision.shape[2]
    part_width = vision.shape[3]
    wanted = image_of[0, lax.axis_index("section")]
    shard_piece = lax.all_gather(vision, "section", axis=1, tiled=True)
    owners = jnp.arange(shard_piece.shape[1])
    chosen = (owners == wanted)[:, None, None]
    taken = jnp.where(chosen, shard_piece[0], jnp.zeros_like(shard_piece[0]))
    image_part = jnp.sum(taken.astype(jnp.float32), axis=0).astype(jnp.bfloat16)
    image = lax.all_gather(image_part, "mp", axis=1, tiled=True)
    width_k = key_full.shape[1]
    keys_raw = jnp.dot(image, key_full, preferred_element_type=jnp.float32).reshape(
        slot_rows, width_k // HD, HD
    )
    values_raw = jnp.dot(image, value_full, preferred_element_type=jnp.float32).reshape(
        slot_rows, width_k // HD, HD
    )
    usable = jnp.arange(slot_rows) < tile_counts[0, wanted] * TILE_ROWS
    present = jnp.arange(text_rows) < lengths[0, 0]

    def forward(keys_in, values_in):
        return attend(queries, keys_in, values_in, key_gain[0], usable, present, cross_gate[0])

    context, pullback = jax.vjp(forward, keys_raw, values_raw)
    gated_context = context.astype(jnp.bfloat16).reshape(1, 1, text_rows, width_q)
    key_back, value_back = pullback(context_grad[0, 0].astype(jnp.float32))
    key_flat = key_back.reshape(slot_rows, width_k).astype(jnp.bfloat16)
    value_flat = value_back.reshape(slot_rows, width_k).astype(jnp.bfloat16)
    contract = (((1,), (1,)), ((), ()))
    partial_sum = lax.dot_general(key_flat, key_full, contract, preferred_element_type=jnp.float32)
    partial_sum = partial_sum + lax.dot_general(
        value_flat, value_full, contract, preferred_element_type=jnp.float32
    )
    partial_bf = partial_sum.astype(jnp.bfloat16)
    summed = lax.psum_scatter(
        partial_bf.astype(jnp.float32).astype(jnp.bfloat16), "mp", scatter_dimension=1, tiled=True
    )
    row_ids = jnp.arange(slot_rows * lax.axis_size("section"))
    taken = jnp.take(summed, row_ids % slot_rows, axis=0).astype(jnp.float32)
    routed = lax.psum_scatter(
        jnp.where((row_ids // slot_rows == wanted)[:, None], taken, 0.0).astype(jnp.bfloat16),
        "section",
        scatter_dimension=0,
        tiled=True,
    )
    vision_grad = routed.reshape(1, 1, slot_rows, part_width)
    columns = image
    inner = (((0,), (0,)), ((), ()))
    key_part = lax.dot_general(columns, key_flat, inner, preferred_element_type=jnp.float32).astype(
        jnp.bfloat16
    )
    value_part = lax.dot_general(
        columns, value_flat, inner, preferred_element_type=jnp.float32
    ).astype(jnp.bfloat16)
    both_grads = lax.psum_scatter(
        jnp.concatenate([key_part, value_part], axis=1).astype(jnp.float32).astype(jnp.bfloat16),
        "dp",
        scatter_dimension=0,
        tiled=True,
    )
    key_weight_grad = both_grads[:, :width_k][None]
    value_weight_grad = both_grads[:, width_k:][None]
    return (gated_context, vision_grad, key_weight_grad, value_weight_grad)


def solution(mesh):
    return jax.shard_map(
        per_device,
        mesh=mesh,
        in_specs=(
            P("dp", "section", None, "mp"),
            P("dp", "section", None, "mp"),
            P("dp", None),
            P("dp", "section"),
            P("dp", None),
            P("section", None),
            P("section", "dp", "mp"),
            P("section", "dp", "mp"),
            P("section", "dp", "mp"),
            P("section", None),
            P("section", None),
            P("section"),
            P("dp", "section", None, "mp"),
        ),
        out_specs=(
            P("dp", "section", None, "mp"),
            P("dp", "section", None, "mp"),
            P("section", "dp", "mp"),
            P("section", "dp", "mp"),
        ),
        check_vma=False,
    )
```

profile of v0, /device:TPU:0, one launch (start us, length us, event | category | flops | bytes accessed | tf_op | source)
XLA Modules:
  0.0 705.0 jit_solution(10474390815657424555)
XLA Ops:
  7.2 0.7 all-gather.7.cloned.1.call-update
  7.9 0.0 all-gather.13.cloned.1.call-start
  8.0 0.7 all-gather.13.cloned.1.call-update
  8.7 0.0 all-gather.11.cloned.1.call-start
  8.7 0.7 all-gather.11.cloned.1.call-update
  9.4 0.0 all-gather.9.cloned.1.call-start
  9.5 0.6 constant_dynamic-slice_fusion.1
  10.0 0.6 iota_compare_fusion.2
  10.7 34.7 %all-gather.7.cloned.1.call-done = bf16[1,2,256,2048]{3,2,0,1:T(8,128)(2,1)} async-done(((bf16[1,1,256,2048]{3,2,0,1:T(8,128)(2,1)}), bf16[1,2,256,2048]{3,2,0,1:T(8,128)(2,1)}) %all-gather.7.cloned.1.call-update) | async-done | bytes 2097168 | tf_op jit(solution)/shard_map/all_gather | solution.py:79
  45.4 3.4 fusion.34
  48.8 0.0 all-gather.15.cloned.1.call-start
  48.9 0.4 collective-permute-start
  49.3 47.3 %collective-permute-done = bf16[1,1,512,2048]{3,2,1,0:T(8,128)(2,1)S(1)} collective-permute-done((bf16[1,1,512,2048]{3,2,1,0:T(8,128)(2,1)}, bf16[1,1,512,2048]{3,2,1,0:T(8,128)(2,1)S(1)}, u32[]{:S(2)}, u32[]{:S(2)}) %collective-permute-start) | collective-permute-done | bytes 2097184 | tf_op jit(solution)/shard_map/ppermute | solution.py:13
  96.5 1.4 copy-done.11
  98.0 0.0 all-gather.17.cloned.1.call-start
  98.0 0.5 all-gather.17.cloned.1.call-update
  98.5 0.0 reduce-scatter.4.cloned.1.call-start
  99.9 0.5 copy.81
  102.4 0.6 fusion.100
  103.0 1.2 iota_compare_fusion.1
  104.2 6.4 copy.51
  110.6 7.0 all-gather.11.cloned.1.call-done
  117.6 6.4 copy.50
  123.9 76.4 %all-gather.9.cloned.1.call-done = bf16[256,8192]{1,0:T(8,128)(2,1)} async-done(((bf16[256,2048]{1,0:T(8,128)(2,1)}), bf16[256,8192]{1,0:T(8,128)(2,1)}) %all-gather.9.cloned.1.call-update) | async-done | bytes 4194320 | tf_op jit(solution)/shard_map/all_gather | solution.py:84
  200.4 4.9 multiply_reduce_fusion.2
  205.3 0.7 multiply_convert_fusion.1
  206.0 0.3 copy-done.10
  206.3 1.3 fusion.60
  207.6 2.0 fusion.43
  209.6 140.3 %all-gather.15.cloned.1.call-done = bf16[1,1,512,8192]{3,2,1,0:T(8,128)(2,1)} async-done(((bf16[1,1,512,2048]{3,2,1,0:T(8,128)(2,1)}), bf16[1,1,512,8192]{3,2,1,0:T(8,128)(2,1)}) %all-gather.15.cloned.1.call-update) | async-done | bytes 8388624 | tf_op jit(solution)/shard_map/all_gather | solution.py:57
  350.0 5.1 fusion.1
  355.1 100.4 %all-gather.17.cloned.1.call-done = bf16[1,8192,1024]{2,1,0:T(8,128)(2,1)} async-done(((bf16[1,2048,1024]{2,1,0:T(8,128)(2,1)}), bf16[1,8192,1024]{2,1,0:T(8,128)(2,1)}) %all-gather.17.cloned.1.call-update) | async-done | bytes 16777232 | tf_op jit(solution)/shard_map/all_gather | solution.py:64
  455.5 21.4 %copy.52 = bf16[1024,8192]{1,0:T(8,128)(2,1)} copy(bf16[1024,8192]{0,1:T(8,128)(2,1)} %bitcast.150) | data formatting | bytes 33554432 | tf_op jit(solution)/shard_map/dot_general | solution.py:62
  477.0 14.8 %multiply_reduce_fusion = (f32[512,8]{0,1:T(8,128)S(1)}, f32[512,8,128]{0,2,1:T(8,128)S(1)}) fusion(bf16[8,128,8192]{2,1,0:T(8,128)(2,1)} %bitcast.151, bf16[1,1,512,8192]{3,2,1,0:T(8,128)(2,1)} %all-gather.15.cloned.1.call-done, f32[8192]{0:T(1024)S(1)} %bitcast.169, f32[512]{0:T(512)S(1)} %add_rsqrt_fusion.1), kind=kOutput, calls=%fused_computation.55 | convolution fusion | flops 8607756288 | bytes 27314176 | tf_op jit(solution)/shard_map/dot_general | solution.py:62
  491.8 0.5 multiply_convert_fusion
  492.3 5.1 fusion.101
  497.4 0.7 multiply_divide_fusion
  498.1 3.9 fusion.16
  502.0 0.7 copy-done.9
  502.8 1.2 fusion.66
  504.0 0.1 multiply_reduce_fusion.1
  504.1 0.1 fusion.75
  504.3 0.8 fusion.63
  505.1 1.1 copy-done.4
  506.2 1.3 fusion.19
  507.5 0.9 copy-done.7
  508.4 3.4 fusion.4
  511.8 0.0 reduce-scatter.8.cloned.1.call-start
  511.9 5.5 convolution_convert_fusion
  517.4 3.2 convolution_convert_fusion.1
  520.6 7.7 %pad_maximum_fusion = bf16[8192,512]{0,1:T(8,128)(2,1)} fusion(bf16[8192,256]{0,1:T(8,128)(2,1)} %convolution_convert_fusion, bf16[8192,256]{0,1:T(8,128)(2,1)} %convolution_convert_fusion.1), kind=kLoop, calls=%fused_computation.13 | loop fusion | flops 16777216 | bytes 16777216 | tf_op jit(solution)/shard_map/concatenate | solution.py:130
  528.3 0.0 reduce-scatter.6.cloned.1.call-start
  528.4 0.7 fusion.89
  529.1 59.6 %reduce-scatter.4.cloned.1.call-done = bf16[256,2048]{1,0:T(8,128)(2,1)} async-done(((bf16[256,8192]{1,0:T(8,128)(2,1)}), bf16[256,2048]{1,0:T(8,128)(2,1)}) %reduce-scatter.4.cloned.1.call-update) | async-done | bytes 1048592 | tf_op jit(solution)/shard_map/reduce_scatter | solution.py:109
  588.7 6.8 gather_fusion
  595.5 3.7 select_convert_fusion
  599.3 0.5 convolution_multiply_fusion
  599.8 0.5 copy.57
  600.3 1.2 select_convert_fusion.1
  601.6 62.2 %reduce-scatter.8.cloned.1.call-done = bf16[2048,512]{0,1:T(8,128)(2,1)} async-done(((bf16[8192,512]{0,1:T(8,128)(2,1)}), bf16[2048,512]{0,1:T(8,128)(2,1)}) %reduce-scatter.8.cloned.1.call-update) | async-done | bytes 2097168 | tf_op jit(solution)/shard_map/reduce_scatter | solution.py:129
  663.8 1.7 slice_bitcast_fusion
  665.4 1.3 copy.64
  666.7 1.3 copy.65
  668.0 30.4 %reduce-scatter.6.cloned.1.call-done = bf16[256,2048]{1,0:T(8,128)(2,1)} async-done(((bf16[512,2048]{1,0:T(8,128)(2,1)}), bf16[256,2048]{1,0:T(8,128)(2,1)}) %reduce-scatter.6.cloned.1.call-update) | async-done | bytes 1048592 | tf_op jit(solution)/shard_map/reduce_scatter | solution.py:114
  (49 shorter events, 0.3 us)
Async XLA Ops:
  7.2 2.3 copy-start
  7.2 38.2 %all-gather.7.cloned.1.call-start = ((), (), s32[]{:S(2)}) async-start(), calls=%async_computation.3 | async-start | bytes 3145728 | tf_op jit(solution)/shard_map/all_gather | solution.py:79
  7.9 96.3 %all-gather.13.cloned.1.call-start = ((), (), s32[]{:S(2)}) async-start(), calls=%async_computation.6 | async-start | bytes 5242880 | tf_op jit(solution)/shard_map/all_gather | solution.py:71
  8.7 108.9 %all-gather.11.cloned.1.call-start = ((), (), s32[]{:S(2)}) async-start(), calls=%async_computation.5 | async-start | bytes 5242880 | tf_op jit(solution)/shard_map/all_gather | solution.py:72
  9.4 191.0 %all-gather.9.cloned.1.call-start = ((), (), s32[]{:S(2)}) async-start(), calls=%async_computation.4 | async-start | bytes 5242880 | tf_op jit(solution)/shard_map/all_gather | solution.py:84
  48.8 51.1 %copy-start.12 = (bf16[1,1,512,1024]{3,2,1,0:T(8,128)(2,1)S(1)}, bf16[1,1,512,1024]{3,2,1,0:T(8,128)(2,1)}, u32[]{:S(2)}) copy-start(bf16[1,1,512,1024]{3,2,1,0:T(8,128)(2,1)} %param.25) | copy-start | bytes 3145732
  48.8 301.2 %all-gather.15.cloned.1.call-start = ((), (), s32[]{:S(2)}) async-start(), calls=%async_computation.7 | async-start | bytes 10485760 | tf_op jit(solution)/shard_map/all_gather | solution.py:57
  48.9 47.6 %collective-permute-start = (bf16[1,1,512,2048]{3,2,1,0:T(8,128)(2,1)}, bf16[1,1,512,2048]{3,2,1,0:T(8,128)(2,1)S(1)}, u32[]{:S(2)}, u32[]{:S(2)}) collective-permute-start(bf16[1,1,512,2048]{3,2,1,0:T(8,128)(2,1)} %param.13), channel_id=1, source_target_pairs={{0,16},{16,0},{1,17},{17,1},{2,18},{18,2},{3,19},{19,3},{4,20},{20... | collective-permute-start | bytes 6291464 | tf_op jit(solution)/shard_map/ppermute | solution.py:13
  96.5 1.4 copy-start.11
  97.9 4.5 copy-start.17
  98.0 357.6 %all-gather.17.cloned.1.call-start = ((), (), s32[]{:S(2)}) async-start(), calls=%async_computation.8 | async-start | bytes 20971520 | tf_op jit(solution)/shard_map/all_gather | solution.py:64
  98.5 490.2 %reduce-scatter.4.cloned.1.call-start = ((), (), s32[]{:S(2)}) async-start(), calls=%async_computation.9 | async-start | bytes 5242880 | tf_op jit(solution)/shard_map/reduce_scatter | solution.py:109
  200.4 4.9 copy-start.14
  200.4 5.7 copy-start.5
  200.4 5.9 copy-start.10
  455.5 21.4 %copy-start.16 = (f32[1,8192]{1,0:T(1,128)S(1)}, f32[1,8192]{1,0:T(1,128)}, u32[]{:S(2)}) copy-start(f32[1,8192]{1,0:T(1,128)} %param.18) | copy-start | bytes 98308
  477.0 14.8 %copy-start.15 = (f32[1,128]{1,0:T(1,128)S(1)}, f32[1,128]{1,0:T(1,128)}, u32[]{:S(2)}) copy-start(f32[1,128]{1,0:T(1,128)} %param.22) | copy-start | bytes 1540
  498.1 3.9 copy-start.8
  498.1 4.7 copy-start.9
  498.1 4.7 copy-start.13
  498.1 4.7 copy-start.18
  502.0 2.3 copy-start.2
  504.0 2.2 copy-start.4
  506.2 2.2 copy-start.7
  511.8 151.9 %reduce-scatter.8.cloned.1.call-start = ((), (), s32[]{:S(2)}) async-start(), calls=%async_computation.11 | async-start | bytes 10485760 | tf_op jit(solution)/shard_map/reduce_scatter | solution.py:129
  511.9 5.5 copy-start.6
  528.3 170.1 %reduce-scatter.6.cloned.1.call-start = ((), (), s32[]{:S(2)}) async-start(), calls=%async_computation.10 | async-start | bytes 3145728 | tf_op jit(solution)/shard_map/reduce_scatter | solution.py:114
  595.5 3.7 copy-start.3
  600.3 98.1 %copy-start.1 = (s32[1,2]{1,0:T(1,128)S(1)}, s32[1,2]{1,0:T(1,128)}, u32[]{:S(2)}) copy-start(s32[1,2]{1,0:T(1,128)} %param.17) | copy-start | bytes 28
Sparse Core Ops, SparseCore 0:
  9.6 35.7 all-gather.6
  47.0 34.4 all-gather.12
  83.1 34.4 all-gather.10
  119.6 80.7 all-gather.8
  201.8 148.1 all-gather.14
  351.4 104.1 all-gather.16
  511.9 76.7 reduce-scatter.3
  591.5 72.2 reduce-scatter.7
  666.6 31.8 reduce-scatter.5
where the time goes:
time: 706 us; the launch traced here: 705 us
  waiting for transfers between devices  561 us (79%)
  local copies, waits for them, and re-layouts  51.3 us (7%)
  matrix products  44.1 us (6%)
  other arithmetic  30.3 us (4%)
  between operations  17.4 us (2%)
    all_gather x1, waiting for transfers between devices, per_device(): full_text = lax.all_gather(arrived, 'mp', axis=3, tiled=True)[0, 0]  140 us
    all_gather x1, waiting for transfers between devices, per_device(): lax.all_gather(query_weight, 'dp', axis=1, tiled=True)[0]  100 us
    all_gather x1, waiting for transfers between devices, per_device(): image = lax.all_gather(image_part, 'mp', axis=1, tiled=True)  76.4 us
    reduce_scatter x1, waiting for transfers between devices, per_device(): lax.psum_scatter(jnp.concatenate([key_part, value_part], axis=1).astype(j...  62.2 us
    reduce_scatter x1, waiting for transfers between devices, per_device(): lax.psum_scatter(partial_bf.astype(jnp.float32).astype(jnp.bfloat16), 'mp...  59.6 us
    ppermute x1, waiting for transfers between devices, shifted(): return lax.ppermute(value, axis, pairs)  47.3 us
    all_gather x1, waiting for transfers between devices, per_device(): shard_piece = lax.all_gather(vision, 'section', axis=1, tiled=True)  34.7 us
    reduce_scatter x1, waiting for transfers between devices, per_device(): lax.psum_scatter(jnp.where((row_ids // slot_rows == wanted)[:, None], tak...  30.4 us
  transfers between devices with their start and end apart: 10, of which 9 were waited for; matrix products, arithmetic and copies ran while one was open for 10% of the time, Pallas kernels for 0%

commit v1 on v0

--- a/solution.py
+++ b/solution.py
@@ -5,6 +5,19 @@
 
 HD = 128
 TILE_ROWS = 64
+
+
+def ring_gather(x, axis, dim):
+    ways = lax.axis_size(axis)
+    up = [(d, (d + 1) % ways) for d in range(ways)]
+    down = [(d, (d - 1) % ways) for d in range(ways)]
+    earlier, later = ([x], [x])
+    for _ in range(ways // 2):
+        earlier.append(lax.ppermute(earlier[-1], axis, up))
+    for _ in range((ways - 1) // 2):
+        later.append(lax.ppermute(later[-1], axis, down))
+    line = jnp.concatenate([*earlier[::-1], *later[1:]], axis=dim)
+    return jnp.roll(line, (lax.axis_index(axis) - ways // 2) * x.shape[dim], axis=dim)
 
 
 def shifted(value, axis, steps):
@@ -54,7 +67,7 @@
     context_grad,
 ):
     arrived = shifted(text_in, "section", 1)
-    full_text = lax.all_gather(arrived, "mp", axis=3, tiled=True)[0, 0]
+    full_text = ring_gather(arrived, "mp", 3)[0, 0]
     text_rows = full_text.shape[0]
     normed = norm_rows(full_text, norm_gain[0]).astype(jnp.bfloat16)
     width_q = query_weight.shape[2]

time: 706 us -> 635 us (0.90)
  waiting for transfers between devices: 561 us -> 453 us
  starting transfers between devices: 0.74 us -> 22.1 us
  local copies, waits for them, and re-layouts: 51.3 us -> 69.4 us
    ppermute x0 -> x3, waiting for transfers between devices: none -> 174 us  [the longest x2 138 us: ring_gather(): earlier.append(lax.ppermute(earlier[-1], axis, up))]
    all_gather x1 -> x0, waiting for transfers between devices: 140 us -> none  [per_device(): full_text = lax.all_gather(arrived, 'mp', axis=3, tiled=True)[0, 0]]
    all_gather x1, waiting for transfers between devices: 76.4 us -> 0.01 us  [per_device(): image = lax.all_gather(image_part, 'mp', axis=1, tiled=True)]
    all_gather x1, waiting for transfers between devices: 100 us -> 42.8 us  [per_device(): lax.all_gather(query_weight, 'dp', axis=1, tiled=True)[0]]
    ppermute x0 -> x3, starting transfers between devices: none -> 21.4 us  [the longest x2 16.2 us: ring_gather(): earlier.append(lax.ppermute(earlier[-1], axis, up))]
    unnamed x40 -> x49, local copies, waits for them, and re-layouts: 6.98 us -> 23.4 us
  transfers between devices with their start and end apart: 10 -> 12, of which waited for: 9 -> 9; matrix products, arithmetic and copies ran while one was open for 10% -> 12% of each run, Pallas kernels for 0% -> 0%
where the time goes in v1:
time: 635 us; the launch traced here: 634 us
  waiting for transfers between devices  453 us (71%)
  local copies, waits for them, and re-layouts  69.4 us (11%)
  matrix products  44.1 us (7%)
  other arithmetic  26.9 us (4%)
  starting transfers between devices  22.1 us (3%)
  between operations  17.8 us (3%)
    ppermute x2, waiting for transfers between devices, ring_gather(): earlier.append(lax.ppermute(earlier[-1], axis, up))  138 us
    reduce_scatter x1, waiting for transfers between devices, per_device(): lax.psum_scatter(jnp.concatenate([key_part, value_part], axis=1).astype(j...  62.1 us
    reduce_scatter x1, waiting for transfers between devices, per_device(): lax.psum_scatter(partial_bf.astype(jnp.float32).astype(jnp.bfloat16), 'mp...  59.6 us
    ppermute x1, waiting for transfers between devices, shifted(): return lax.ppermute(value, axis, pairs)  47.2 us
    all_gather x1, waiting for transfers between devices, per_device(): lax.all_gather(query_weight, 'dp', axis=1, tiled=True)[0]  42.8 us
    ppermute x1, waiting for transfers between devices, ring_gather(): later.append(lax.ppermute(later[-1], axis, down))  35.8 us
    all_gather x1, waiting for transfers between devices, per_device(): shard_piece = lax.all_gather(vision, 'section', axis=1, tiled=True)  34.7 us
    reduce_scatter x1, waiting for transfers between devices, per_device(): lax.psum_scatter(jnp.where((row_ids // slot_rows == wanted)[:, None], tak...  30.4 us
  transfers between devices with their start and end apart: 12, of which 9 were waited for; matrix products, arithmetic and copies ran while one was open for 12% of the time, Pallas kernels for 0%

profile of v1, /device:TPU:0, one launch (start us, length us, event | category | flops | bytes accessed | tf_op | source)
XLA Modules:
  0.0 633.5 jit_solution(2979386620248394380)
XLA Ops:
  7.2 0.7 all-gather.6.cloned.1.call-update
  8.0 0.7 all-gather.12.cloned.1.call-update
  8.7 0.7 all-gather.10.cloned.1.call-update
  9.5 0.6 constant_dynamic-slice_fusion.1
  10.0 0.6 iota_compare_fusion.2
  10.7 34.7 %all-gather.6.cloned.1.call-done = bf16[1,2,256,2048]{3,2,0,1:T(8,128)(2,1)} async-done(((bf16[1,1,256,2048]{3,2,0,1:T(8,128)(2,1)}), bf16[1,2,256,2048]{3,2,0,1:T(8,128)(2,1)}) %all-gather.6.cloned.1.call-update) | async-done | bytes 2097168 | tf_op jit(solution)/shard_map/all_gather | solution.py:92
  45.4 3.4 fusion.35
  48.9 0.5 all-gather.14.cloned.1.call-update
  49.5 0.4 collective-permute-start
  49.9 47.2 %collective-permute-done = bf16[1,1,512,2048]{3,2,1,0:T(8,128)(2,1)} collective-permute-done((bf16[1,1,512,2048]{3,2,1,0:T(8,128)(2,1)S(1)}, bf16[1,1,512,2048]{3,2,1,0:T(8,128)(2,1)}, u32[]{:S(2)}, u32[]{:S(2)}) %collective-permute-start) | collective-permute-done | bytes 2097184 | tf_op jit(solution)/shard_map/ppermute | solution.py:26
  97.0 1.5 collective-permute-start.1
  98.5 62.3 %collective-permute-done.1 = bf16[1,1,512,2048]{3,2,1,0:T(8,128)(2,1)} collective-permute-done((bf16[1,1,512,2048]{3,2,1,0:T(8,128)(2,1)}, bf16[1,1,512,2048]{3,2,1,0:T(8,128)(2,1)}, u32[]{:S(2)}, u32[]{:S(2)}) %collective-permute-start.1) | collective-permute-done | bytes 2097184 | tf_op jit(solution)/shard_map/ppermute | solution.py:16
  160.8 14.7 %collective-permute-start.2 = (bf16[1,1,512,2048]{3,2,1,0:T(8,128)(2,1)}, bf16[1,1,512,2048]{3,2,1,0:T(8,128)(2,1)}, u32[]{:S(2)}, u32[]{:S(2)}) collective-permute-start(bf16[1,1,512,2048]{3,2,1,0:T(8,128)(2,1)} %collective-permute-done.1), channel_id=1, source_target_pairs={{0,4},{4,8},{8,12},{12,0},{1,5},{5,9},{9,13},{13,1},{2,6},{6,10},{... | collective-permute-start | bytes 6291464 | tf_op jit(solution)/shard_map/ppermute | solution.py:16
  175.6 5.1 collective-permute-start.3
  183.3 0.5 copy.81
  184.6 0.6 fusion.102
  185.1 1.2 iota_compare_fusion.1
  186.3 75.6 %collective-permute-done.2 = bf16[1,1,512,2048]{3,2,1,0:T(8,128)(2,1)} collective-permute-done((bf16[1,1,512,2048]{3,2,1,0:T(8,128)(2,1)}, bf16[1,1,512,2048]{3,2,1,0:T(8,128)(2,1)}, u32[]{:S(2)}, u32[]{:S(2)}) %collective-permute-start.2) | collective-permute-done | bytes 2097184 | tf_op jit(solution)/shard_map/ppermute | solution.py:16
  261.9 1.7 constant_dynamic-update-slice_fusion.7
  263.7 1.7 constant_dynamic-update-slice_fusion.6
  265.4 1.7 constant_dynamic-update-slice_fusion.5
  267.1 35.8 %collective-permute-done.3 = bf16[1,1,512,2048]{3,2,1,0:T(8,128)(2,1)} collective-permute-done((bf16[1,1,512,2048]{3,2,1,0:T(8,128)(2,1)}, bf16[1,1,512,2048]{3,2,1,0:T(8,128)(2,1)}, u32[]{:S(2)}, u32[]{:S(2)}) %collective-permute-start.3) | collective-permute-done | bytes 2097184 | tf_op jit(solution)/shard_map/ppermute | solution.py:18
  302.9 1.7 constant_dynamic-update-slice_fusion.4
  304.7 1.7 constant_dynamic-update-slice_fusion.3
  306.4 1.7 constant_dynamic-update-slice_fusion.2
  308.1 1.7 constant_dynamic-update-slice_fusion.1
  309.9 1.7 constant_dynamic-update-slice_fusion
  311.6 5.7 copy-done.9
  317.3 1.7 fusion.1
  319.1 6.4 %copy.51 = bf16[256,8192]{1,0:T(8,128)(2,1)} copy(bf16[256,8192]{0,1:T(8,128)(2,1)} %bitcast.149) | data formatting | bytes 8388608 | tf_op jit(solution)/shard_map/dot_general | solution.py:99
  325.5 6.4 %copy.50 = bf16[256,8192]{1,0:T(8,128)(2,1)} copy(bf16[256,8192]{0,1:T(8,128)(2,1)} %bitcast.152) | data formatting | bytes 8388608 | tf_op jit(solution)/shard_map/dot_general | solution.py:102
  331.9 4.9 multiply_reduce_fusion.2
  336.8 0.7 multiply_convert_fusion.1
  337.9 1.3 fusion.61
  339.1 2.1 fusion.44
  341.2 42.8 %all-gather.14.cloned.1.call-done = bf16[1,8192,1024]{2,1,0:T(8,128)(2,1)} async-done(((bf16[1,2048,1024]{2,1,0:T(8,128)(2,1)}), bf16[1,8192,1024]{2,1,0:T(8,128)(2,1)}) %all-gather.14.cloned.1.call-update) | async-done | bytes 16777232 | tf_op jit(solution)/shard_map/all_gather | solution.py:77
  384.1 21.2 %copy.52 = bf16[1024,8192]{1,0:T(8,128)(2,1)} copy(bf16[1024,8192]{0,1:T(8,128)(2,1)} %bitcast.150) | data formatting | bytes 33554432 | tf_op jit(solution)/shard_map/dot_general | solution.py:75
  405.3 14.8 %multiply_reduce_fusion = (f32[512,8]{0,1:T(8,128)S(1)}, f32[512,8,128]{0,2,1:T(8,128)S(1)}) fusion(bf16[8,128,8192]{2,1,0:T(8,128)(2,1)} %bitcast.151, f32[8192]{0:T(1024)S(1)} %bitcast.169, f32[512]{0:T(512)S(1)} %add_rsqrt_fusion.1, bf16[1,1,512,16384]{3,2,1,0:T(8,128)(2,1)} %copy-done.9, s32[]{:T(128)S(6)} %select_n.103), kind=kOutput, calls=%fused_computation.56 | convolution fusion | flops 8607756288 | bytes 27314180 | tf_op jit(solution)/shard_map/dot_general | solution.py:75
  420.1 0.5 multiply_convert_fusion
  420.6 5.1 fusion.103
  425.7 0.7 multiply_divide_fusion
  426.5 3.9 fusion.17
  430.4 0.7 copy-done.10
  431.1 1.2 fusion.67
  432.6 0.9 fusion.64
  433.5 1.0 copy-done.4
  434.5 1.3 fusion.20
  435.8 0.9 copy-done.7
  436.7 3.4 fusion.4
  440.2 5.5 convolution_convert_fusion.1
  445.7 3.2 convolution_convert_fusion
  448.9 7.7 %pad_maximum_fusion = bf16[8192,512]{0,1:T(8,128)(2,1)} fusion(bf16[8192,256]{0,1:T(8,128)(2,1)} %convolution_convert_fusion, bf16[8192,256]{0,1:T(8,128)(2,1)} %convolution_convert_fusion.1), kind=kLoop, calls=%fused_computation.13 | loop fusion | flops 16777216 | bytes 16777216 | tf_op jit(solution)/shard_map/concatenate | solution.py:143
  456.7 0.7 fusion.90
  457.4 59.6 %reduce-scatter.4.cloned.1.call-done = bf16[256,2048]{1,0:T(8,128)(2,1)} async-done(((bf16[256,8192]{1,0:T(8,128)(2,1)}), bf16[256,2048]{1,0:T(8,128)(2,1)}) %reduce-scatter.4.cloned.1.call-update) | async-done | bytes 1048592 | tf_op jit(solution)/shard_map/reduce_scatter | solution.py:122
  517.0 6.8 %gather_fusion = bf16[512,2048]{1,0:T(8,128)(2,1)} fusion(bf16[256,2048]{1,0:T(8,128)(2,1)} %reduce-scatter.4.cloned.1.call-done, s32[1024]{0:T(1024)S(1)} %pad_clamp_fusion), kind=kCustom, calls=%fused_computation | custom fusion | bytes 4196352 | tf_op jit(solution)/shard_map/jit(_take)/gather | solution.py:126
  523.9 3.7 select_convert_fusion
  527.6 0.5 convolution_multiply_fusion
  528.1 0.5 copy.57
  528.7 1.2 select_convert_fusion.1
  529.9 62.1 %reduce-scatter.8.cloned.1.call-done = bf16[2048,512]{0,1:T(8,128)(2,1)} async-done(((bf16[8192,512]{0,1:T(8,128)(2,1)}), bf16[2048,512]{0,1:T(8,128)(2,1)}) %reduce-scatter.8.cloned.1.call-update) | async-done | bytes 2097168 | tf_op jit(solution)/shard_map/reduce_scatter | solution.py:142
  592.0 1.7 slice_bitcast_fusion
  593.7 1.3 copy.64
  595.0 1.3 copy.65
  596.3 30.4 %reduce-scatter.6.cloned.1.call-done = bf16[256,2048]{1,0:T(8,128)(2,1)} async-done(((bf16[512,2048]{1,0:T(8,128)(2,1)}), bf16[256,2048]{1,0:T(8,128)(2,1)}) %reduce-scatter.6.cloned.1.call-update) | async-done | bytes 1048592 | tf_op jit(solution)/shard_map/reduce_scatter | solution.py:127
  (62 shorter events, 1.0 us)
Async XLA Ops:
  7.2 2.3 copy-start
  7.2 38.2 %all-gather.6.cloned.1.call-start = ((), (), s32[]{:S(2)}) async-start(), calls=%async_computation.3 | async-start | bytes 3145728 | tf_op jit(solution)/shard_map/all_gather | solution.py:92
  7.9 311.2 %all-gather.12.cloned.1.call-start = ((), (), s32[]{:S(2)}) async-start(), calls=%async_computation.6 | async-start | bytes 5242880 | tf_op jit(solution)/shard_map/all_gather | solution.py:84
  8.7 316.9 %all-gather.10.cloned.1.call-start = ((), (), s32[]{:S(2)}) async-start(), calls=%async_computation.5 | async-start | bytes 5242880 | tf_op jit(solution)/shard_map/all_gather | solution.py:85
  9.4 322.5 %all-gather.8.cloned.1.call-start = ((), (), s32[]{:S(2)}) async-start(), calls=%async_computation.4 | async-start | bytes 5242880 | tf_op jit(solution)/shard_map/all_gather | solution.py:97
  10.7 38.8 %copy-start.16 = (bf16[1,1,512,2048]{3,2,1,0:T(8,128)(2,1)S(1)}, bf16[1,1,512,2048]{3,2,1,0:T(8,128)(2,1)}, u32[]{:S(2)}) copy-start(bf16[1,1,512,2048]{3,2,1,0:T(8,128)(2,1)} %param.13) | copy-start | bytes 6291460
  10.7 172.6 %copy-start.12 = (bf16[1,1,512,1024]{3,2,1,0:T(8,128)(2,1)S(1)}, bf16[1,1,512,1024]{3,2,1,0:T(8,128)(2,1)}, u32[]{:S(2)}) copy-start(bf16[1,1,512,1024]{3,2,1,0:T(8,128)(2,1)} %param.25) | copy-start | bytes 3145732
  48.8 135.7 %copy-start.18 = (s32[1,2]{1,0:T(1,128)S(1)}, s32[1,2]{1,0:T(1,128)}, u32[]{:S(2)}) copy-start(s32[1,2]{1,0:T(1,128)} %param.15) | copy-start | bytes 28
  48.8 335.2 %all-gather.14.cloned.1.call-start = ((), (), s32[]{:S(2)}) async-start(), calls=%async_computation.7 | async-start | bytes 20971520 | tf_op jit(solution)/shard_map/all_gather | solution.py:77
  49.4 467.6 %reduce-scatter.4.cloned.1.call-start = ((), (), s32[]{:S(2)}) async-start(), calls=%async_computation.8 | async-start | bytes 5242880 | tf_op jit(solution)/shard_map/reduce_scatter | solution.py:122
  49.5 47.5 %collective-permute-start = (bf16[1,1,512,2048]{3,2,1,0:T(8,128)(2,1)S(1)}, bf16[1,1,512,2048]{3,2,1,0:T(8,128)(2,1)}, u32[]{:S(2)}, u32[]{:S(2)}) collective-permute-start(bf16[1,1,512,2048]{3,2,1,0:T(8,128)(2,1)S(1)} %copy-done.16), channel_id=1, source_target_pairs={{0,16},{16,0},{1,17},{17,1},{2,18},{18,2},{3,19},{19,3},{4,20},{20... | collective-permute-start | bytes 6291464 | tf_op jit(solution)/shard_map/ppermute | solution.py:26
  97.0 63.8 %collective-permute-start.1 = (bf16[1,1,512,2048]{3,2,1,0:T(8,128)(2,1)}, bf16[1,1,512,2048]{3,2,1,0:T(8,128)(2,1)}, u32[]{:S(2)}, u32[]{:S(2)}) collective-permute-start(bf16[1,1,512,2048]{3,2,1,0:T(8,128)(2,1)} %collective-permute-done), channel_id=1, source_target_pairs={{0,4},{4,8},{8,12},{12,0},{1,5},{5,9},{9,13},{13,1},{2,6},{6,10},{... | collective-permute-start | bytes 6291464 | tf_op jit(solution)/shard_map/ppermute | solution.py:16
  160.8 101.1 %collective-permute-start.2 = (bf16[1,1,512,2048]{3,2,1,0:T(8,128)(2,1)}, bf16[1,1,512,2048]{3,2,1,0:T(8,128)(2,1)}, u32[]{:S(2)}, u32[]{:S(2)}) collective-permute-start(bf16[1,1,512,2048]{3,2,1,0:T(8,128)(2,1)} %collective-permute-done.1), channel_id=1, source_target_pairs={{0,4},{4,8},{8,12},{12,0},{1,5},{5,9},{9,13},{13,1},{2,6},{6,10},{... | collective-permute-start | bytes 6291464 | tf_op jit(solution)/shard_map/ppermute | solution.py:16
  175.6 127.4 %collective-permute-start.3 = (bf16[1,1,512,2048]{3,2,1,0:T(8,128)(2,1)}, bf16[1,1,512,2048]{3,2,1,0:T(8,128)(2,1)}, u32[]{:S(2)}, u32[]{:S(2)}) collective-permute-start(bf16[1,1,512,2048]{3,2,1,0:T(8,128)(2,1)} %collective-permute-done), channel_id=1, source_target_pairs={{0,12},{4,0},{8,4},{12,8},{1,13},{5,1},{9,5},{13,9},{2,14},{6,2},{... | collective-permute-start | bytes 6291464 | tf_op jit(solution)/shard_map/ppermute | solution.py:18
  311.6 5.7 copy-start.9
  331.9 4.9 copy-start.14
  331.9 5.7 copy-start.5
  331.9 5.9 copy-start.11
  384.1 21.2 %copy-start.17 = (f32[1,8192]{1,0:T(1,128)S(1)}, f32[1,8192]{1,0:T(1,128)}, u32[]{:S(2)}) copy-start(f32[1,8192]{1,0:T(1,128)} %param.18) | copy-start | bytes 98308
  405.3 14.8 %copy-start.15 = (f32[1,128]{1,0:T(1,128)S(1)}, f32[1,128]{1,0:T(1,128)}, u32[]{:S(2)}) copy-start(f32[1,128]{1,0:T(1,128)} %param.22) | copy-start | bytes 1540
  426.4 3.9 copy-start.8
  426.4 4.7 copy-start.10
  426.4 4.7 copy-start.13
  426.4 4.7 copy-start.19
  430.3 2.3 copy-start.2
  432.3 2.2 copy-start.4
  434.5 2.2 copy-start.7
  440.1 151.9 %reduce-scatter.8.cloned.1.call-start = ((), (), s32[]{:S(2)}) async-start(), calls=%async_computation.10 | async-start | bytes 10485760 | tf_op jit(solution)/shard_map/reduce_scatter | solution.py:142
  440.2 5.6 copy-start.6
  456.6 170.1 %reduce-scatter.6.cloned.1.call-start = ((), (), s32[]{:S(2)}) async-start(), calls=%async_computation.9 | async-start | bytes 3145728 | tf_op jit(solution)/shard_map/reduce_scatter | solution.py:127
  523.9 3.7 copy-start.3
  528.7 98.0 %copy-start.1 = (s32[1,2]{1,0:T(1,128)S(1)}, s32[1,2]{1,0:T(1,128)}, u32[]{:S(2)}) copy-start(s32[1,2]{1,0:T(1,128)} %param.17) | copy-start | bytes 28
Sparse Core Ops, SparseCore 0:
  9.6 35.7 all-gather.5
  47.0 34.4 all-gather.11
  83.1 34.4 all-gather.9
  119.6 159.2 all-gather.7
  280.2 103.7 all-gather.13
  440.2 76.7 reduce-scatter.3
  519.8 72.2 reduce-scatter.7
  594.8 31.8 reduce-scatter.5
